TPU v7x, 256 devices: a whole 4x4x8 slice. The times are simulated.
256 devices in a mesh: dp: 16 (over x_hi, y, core), block: 16 (over z, x_lo).
Axes of the slice: x: 4 (x_hi: 2, x_lo: 2; x = x_hi * 2 + x_lo), y: 4, z: 8, core: 2. Of those that a mesh axis runs over, the one named last changes fastest.
Arguments:
- inputs: bfloat16 [128, 128, 32768], P('block', None, 'dp'), may hold values from -6 to 6
- left_factor: bfloat16 [128, 128, 128], P('block'), may hold values from -0.5 to 0.5
- right_factor: bfloat16 [128, 128, 128], P('block'), may hold values from -0.5 to 0.5
- cotangent: bfloat16 [128, 128, 32768], P('block', None, 'dp'), may hold values from -6 to 6
Outputs:
- input_grad: bfloat16 [128, 128, 32768], P('block', None, 'dp')
- left_grad: float32 [128, 128, 128], P('block', 'dp')
- right_grad: float32 [128, 128, 128], P('block', 'dp')
All inputs are finite; a program needn't handle non-finite values.
Results may differ from a plain program's by a relative error of at most 0.0055.
Values may be sent and summed in bfloat16 or wider, within the bound.
No kernel may reach another device: no remote copies, remote signals or barrier semaphores. Data moves between devices by JAX's collectives and lax.ppermute only.
A program may use at most 128 MiB of HBM per device.

v0:
```python
import jax
import jax.numpy as jnp
from jax import lax
from jax.sharding import PartitionSpec as P

CHUNKS = (13, 3)
SPLIT_DP = False


def gelu_slope(values):
    return jax.vjp(jax.nn.gelu, values)[1](jnp.ones_like(values))[0]


def dp_reduce_scatter(terms):
    n_dp = lax.axis_size("dp")
    received = lax.all_to_all(terms, "dp", split_axis=2, concat_axis=0, tiled=True)
    received = received.reshape(
        (n_dp,) + terms.shape[:2] + (terms.shape[2] // n_dp,) + terms.shape[3:]
    )
    return jnp.sum(received, axis=0)


def local(inputs, left_factor, right_factor, cotangent):
    tokens_local = inputs.shape[2]
    scale = float(lax.axis_size("dp") * tokens_local) ** (-0.5)
    total = sum(CHUNKS)
    bounds = [0]
    for share in CHUNKS:
        bounds.append(bounds[-1] + tokens_local * share // total)
    input_pieces = []
    grad_left = None
    grad_right = None
    right_done = None
    for group in range(len(CHUNKS)):
        lo, hi = (bounds[group], bounds[group + 1])
        x_group = inputs[:, :, lo:hi]
        dy_group = cotangent[:, :, lo:hi]
        outgoing = jnp.einsum(
            "ict,ico->oit", x_group, left_factor, preferred_element_type=jnp.float32
        ).astype(jnp.bfloat16)
        forward_received = lax.all_to_all(
            outgoing, "block", split_axis=0, concat_axis=1, tiled=True
        )
        mixed = jnp.einsum(
            "jit,jik->jkt", forward_received, right_factor, preferred_element_type=jnp.float32
        )
        slope = gelu_slope(mixed)
        mixed_grad = (dy_group.astype(jnp.float32) * slope).astype(jnp.bfloat16)
        right_term = (
            jnp.einsum(
                "jit,jkt->jik", forward_received, mixed_grad, preferred_element_type=jnp.float32
            )
            * scale
        )
        grad_right = right_term if grad_right is None else grad_right + right_term
        if SPLIT_DP and group == len(CHUNKS) - 1:
            right_done = dp_reduce_scatter(grad_right[None])[0]
        permuted_grad = jnp.einsum(
            "jkt,jik->jit", mixed_grad, right_factor, preferred_element_type=jnp.float32
        ).astype(jnp.bfloat16)
        received = lax.all_to_all(permuted_grad, "block", split_axis=1, concat_axis=0, tiled=True)
        branch = jnp.einsum(
            "oit,ico->ict", received, left_factor, preferred_element_type=jnp.float32
        )
        residual = dy_group.astype(jnp.float32)
        input_pieces.append((residual + branch).astype(jnp.bfloat16))
        left_term = (
            jnp.einsum("ict,oit->ico", x_group, received, preferred_element_type=jnp.float32)
            * scale
        )
        grad_left = left_term if grad_left is None else grad_left + left_term
    input_grad = jnp.concatenate(input_pieces, axis=2)
    if SPLIT_DP:
        return (input_grad, dp_reduce_scatter(grad_left[None])[0], right_done)
    reduced = dp_reduce_scatter(jnp.stack([grad_left, grad_right]))
    return (input_grad, reduced[0], reduced[1])


def solution(mesh):
    placed = (
        P("block", None, "dp"),
        P("block", None, None),
        P("block", None, None),
        P("block", None, "dp"),
    )
    return jax.shard_map(
        local,
        mesh=mesh,
        in_specs=placed,
        out_specs=(P("block", None, "dp"), P("block", "dp", None), P("block", "dp", None)),
        check_vma=False,
    )
```

profile of v0, /device:TPU:1, one launch (start us, length us, event | category | flops | bytes accessed | tf_op | source)
XLA Modules:
  0.0 259.9 jit_solution(1413870222509505531)
XLA Ops:
  0.6 0.0 copy-start
  0.6 0.0 copy-start.4
  0.7 1.7 fusion.30
  2.3 1.3 copy.85
  3.7 10.0 %all-to-all-start.2 = ((bf16[128,8,384]{2,1,0:T(8,128)(2,1)}), bf16[128,8,384]{2,1,0:T(8,128)(2,1)S(1)}, u32[]{:S(2)}, u32[]{:S(2)}) async-start(bf16[128,8,384]{2,1,0:T(8,128)(2,1)} %copy.85), calls=%async_computation.2 | async-start | bytes 1572864 | tf_op jit(solution)/shard_map/all_to_all | solution.py:41
  13.7 3.1 %fusion.12 = bf16[128,8,1664]{2,0,1:T(8,128)(2,1)S(1)} fusion(bf16[8,128,128]{2,1,0:T(8,128)(2,1)S(1)} %copy-done.4, bf16[8,128,2048]{2,1,0:T(8,128)(2,1)} %param.4), kind=kOutput, calls=%fused_computation.20 | convolution fusion | flops 437911552 | bytes 7077888 | tf_op jit(solution)/shard_map/ict,ico->oit/dot_general | solution.py:38
  16.8 3.7 %copy.76 = bf16[128,8,1664]{2,1,0:T(8,128)(2,1)} copy(bf16[128,8,1664]{2,0,1:T(8,128)(2,1)S(1)} %fusion.12) | data formatting | bytes 6815744 | tf_op jit(solution)/shard_map/convert_element_type | solution.py:40
  20.5 14.0 %all-to-all-done.2 = bf16[128,8,384]{2,1,0:T(8,128)(2,1)S(1)} async-done(((bf16[128,8,384]{2,1,0:T(8,128)(2,1)}), bf16[128,8,384]{2,1,0:T(8,128)(2,1)S(1)}, u32[]{:S(2)}, u32[]{:S(2)}) %all-to-all-start.2) | async-done | bytes 786464 | tf_op jit(solution)/shard_map/all_to_all | solution.py:41
  34.5 0.9 copy-done.8
  35.4 5.3 %all-to-all-start = ((bf16[128,8,1664]{2,1,0:T(8,128)(2,1)}), bf16[128,8,1664]{2,1,0:T(8,128)(2,1)}, u32[]{:S(2)}, u32[]{:S(2)}) async-start(bf16[128,8,1664]{2,1,0:T(8,128)(2,1)} %copy.76), calls=%async_computation | async-start | bytes 6815744 | tf_op jit(solution)/shard_map/all_to_all | solution.py:41
  40.7 0.0 slice-start
  40.7 4.1 %slice.18 = bf16[8,128,1664]{2,1,0:T(8,128)(2,1)} slice(bf16[8,128,2048]{2,1,0:T(8,128)(2,1)} %param.7), slice={[0:8], [0:128], [0:1664]} | slice | bytes 6815744 | tf_op jit(solution)/shard_map/slice | solution.py:37
  44.8 0.0 slice-done
  44.8 0.4 copy.114
  45.2 5.9 %copy.113 = bf16[8,128,1664]{1,2,0:T(8,128)(2,1)} copy(bf16[8,128,1664]{2,1,0:T(8,128)(2,1)} %slice.18) | data formatting | bytes 6815744
  51.1 0.0 copy-done
  51.1 1.3 fusion.21
  52.4 0.4 fusion.31
  52.8 1.3 copy.88
  54.1 64.7 %all-to-all-done = bf16[128,8,1664]{2,1,0:T(8,128)(2,1)} async-done(((bf16[128,8,1664]{2,1,0:T(8,128)(2,1)}), bf16[128,8,1664]{2,1,0:T(8,128)(2,1)}, u32[]{:S(2)}, u32[]{:S(2)}) %all-to-all-start) | async-done | bytes 3407904 | tf_op jit(solution)/shard_map/all_to_all | solution.py:41
  118.9 4.1 %all-to-all-start.3 = ((bf16[8,128,384]{2,0,1:T(8,128)(2,1)}), bf16[8,128,384]{2,0,1:T(8,128)(2,1)S(1)}, u32[]{:S(2)}, u32[]{:S(2)}) async-start(bf16[8,128,384]{2,0,1:T(8,128)(2,1)} %copy.88), calls=%async_computation.3 | async-start | bytes 1572864 | tf_op jit(solution)/shard_map/all_to_all | solution.py:61
  123.0 7.6 %fusion = bf16[8,128,1664]{1,2,0:T(8,128)(2,1)S(1)} fusion(bf16[8,128,1664]{1,2,0:T(8,128)(2,1)} %copy.113, bf16[8,128,128]{2,1,0:T(8,128)(2,1)S(1)} %copy-done, bf16[8,16,8,1664]{3,2,0,1:T(8,128)(2,1)} %bitcast.2), kind=kOutput, calls=%fused_computation.4 | convolution fusion | flops 470286336 | bytes 10485760 | tf_op jit(solution)/shard_map/jit,jik->jkt/dot_general | solution.py:44
  130.6 0.0 copy-start.5
  130.6 1.7 copy-done.5
  132.3 2.8 %fusion.13 = bf16[8,128,1664]{1,2,0:T(8,128)(2,1)} fusion(bf16[8,128,1664]{1,2,0:T(8,128)(2,1)S(1)} %fusion, bf16[8,128,128]{2,1,0:T(8,128)(2,1)S(1)} %copy-done), kind=kOutput, calls=%fused_computation.21 | convolution fusion | flops 437911552 | bytes 7077888 | tf_op jit(solution)/shard_map/jkt,jik->jit/dot_general | solution.py:58
  135.1 6.0 %copy.79 = bf16[8,128,1664]{2,0,1:T(8,128)(2,1)} copy(bf16[8,128,1664]{1,2,0:T(8,128)(2,1)} %fusion.13) | data formatting | bytes 6815744 | tf_op jit(solution)/shard_map/convert_element_type | solution.py:60
  141.0 2.5 all-to-all-done.3
  143.5 5.5 %all-to-all-start.1 = ((bf16[8,128,1664]{2,0,1:T(8,128)(2,1)}), bf16[8,128,1664]{2,0,1:T(8,128)(2,1)}, u32[]{:S(2)}, u32[]{:S(2)}) async-start(bf16[8,128,1664]{2,0,1:T(8,128)(2,1)} %copy.79), calls=%async_computation.1 | async-start | bytes 6815744 | tf_op jit(solution)/shard_map/all_to_all | solution.py:61
  149.1 0.1 copy.90
  149.2 4.3 %fusion.9 = f32[8,128,128]{1,2,0:T(8,128)S(1)} fusion(bf16[8,128,1664]{1,2,0:T(8,128)(2,1)} %copy-done.5, bf16[8,16,8,1664]{3,2,0,1:T(8,128)(2,1)} %bitcast.2), kind=kOutput, calls=%fused_computation.17 | convolution fusion | flops 436207616 | bytes 7340032 | tf_op jit(solution)/shard_map/jit,jkt->jik/dot_general | solution.py:50
  153.6 1.3 fusion.35
  154.8 72.4 %all-to-all-done.1 = bf16[8,128,1664]{2,0,1:T(8,128)(2,1)} async-done(((bf16[8,128,1664]{2,0,1:T(8,128)(2,1)}), bf16[8,128,1664]{2,0,1:T(8,128)(2,1)}, u32[]{:S(2)}, u32[]{:S(2)}) %all-to-all-start.1) | async-done | bytes 3407904 | tf_op jit(solution)/shard_map/all_to_all | solution.py:61
  227.3 2.6 %copy.81 = bf16[16,8,8,1664]{3,2,1,0:T(8,128)(2,1)S(1)} copy(bf16[16,8,8,1664]{3,1,2,0:T(8,128)(2,1)} %bitcast.8) | data formatting | bytes 6815744 | tf_op jit(solution)/shard_map/all_to_all | solution.py:61
  229.9 0.0 copy-start.2
  229.9 0.6 copy-done.3
  230.5 1.2 fusion.15
  231.7 0.5 fusion.33
  232.2 0.1 pad_maximum_fusion.1
  232.3 1.4 copy.99
  233.7 8.4 %all-to-all-start.4 = ((f32[2,8,128,128]{3,1,0,2:T(8,128)}), f32[2,8,128,128]{3,1,0,2:T(8,128)S(1)}, u32[]{:S(2)}, u32[]{:S(2)}) async-start(f32[2,8,128,128]{3,1,0,2:T(8,128)} %copy.99), calls=%async_computation.4 | async-start | bytes 2097152 | tf_op jit(solution)/shard_map/all_to_all | solution.py:16
  242.1 0.4 fusion.22
  242.6 4.7 %fusion.1 = bf16[8,128,1664]{1,2,0:T(8,128)(2,1)S(1)} fusion(bf16[8,128,1664]{1,2,0:T(8,128)(2,1)} %copy.113, bf16[8,128,128]{2,1,0:T(8,128)(2,1)S(1)} %copy-done.4, bf16[128,8,1664]{2,1,0:T(8,128)(2,1)} %bitcast.82), kind=kOutput, calls=%fused_computation.5 | convolution fusion | flops 441319424 | bytes 10485760 | tf_op jit(solution)/shard_map/oit,ico->ict/dot_general | solution.py:62
  247.3 0.0 copy-start.1
  247.3 2.2 pad_maximum_fusion
  249.5 6.4 %copy.101 = bf16[8,128,2048]{2,1,0:T(8,128)(2,1)} copy(bf16[8,128,2048]{1,2,0:T(8,128)(2,1)} %pad_maximum_fusion) | data formatting | bytes 8388608
  256.0 3.3 %all-to-all-done.4 = f32[2,8,128,128]{3,1,0,2:T(8,128)S(1)} async-done(((f32[2,8,128,128]{3,1,0,2:T(8,128)}), f32[2,8,128,128]{3,1,0,2:T(8,128)S(1)}, u32[]{:S(2)}, u32[]{:S(2)}) %all-to-all-start.4) | async-done | bytes 1048608 | tf_op jit(solution)/shard_map/all_to_all | solution.py:16
  259.2 0.1 reduce.2
  259.3 0.6 copy_bitcast_fusion
  (16 shorter events, 0.0 us)
Async XLA Ops:
  0.6 50.4 %copy-start = (bf16[8,128,128]{2,1,0:T(8,128)(2,1)S(1)}, bf16[8,128,128]{2,1,0:T(8,128)(2,1)}, u32[]{:S(2)}) copy-start(bf16[8,128,128]{2,1,0:T(8,128)(2,1)} %param.6) | copy-start | bytes 786436
  0.6 13.1 %copy-start.4 = (bf16[8,128,128]{2,1,0:T(8,128)(2,1)S(1)}, bf16[8,128,128]{2,1,0:T(8,128)(2,1)}, u32[]{:S(2)}) copy-start(bf16[8,128,128]{2,1,0:T(8,128)(2,1)} %param.5) | copy-start | bytes 786436
  3.7 30.8 %all-to-all-start.2 = ((bf16[128,8,384]{2,1,0:T(8,128)(2,1)}), bf16[128,8,384]{2,1,0:T(8,128)(2,1)S(1)}, u32[]{:S(2)}, u32[]{:S(2)}) async-start(bf16[128,8,384]{2,1,0:T(8,128)(2,1)} %copy.85), calls=%async_computation.2 | async-start | bytes 1572864 | tf_op jit(solution)/shard_map/all_to_all | solution.py:41
  34.5 0.9 copy-start.8
  35.4 83.5 %all-to-all-start = ((bf16[128,8,1664]{2,1,0:T(8,128)(2,1)}), bf16[128,8,1664]{2,1,0:T(8,128)(2,1)}, u32[]{:S(2)}, u32[]{:S(2)}) async-start(bf16[128,8,1664]{2,1,0:T(8,128)(2,1)} %copy.76), calls=%async_computation | async-start | bytes 6815744 | tf_op jit(solution)/shard_map/all_to_all | solution.py:41
  40.7 4.1 %slice-start = ((bf16[8,128,2048]{2,1,0:T(8,128)(2,1)}), bf16[8,128,384]{2,1,0:T(8,128)(2,1)S(1)}, s32[]{:S(2)}) async-start(bf16[8,128,2048]{2,1,0:T(8,128)(2,1)} %param.7), calls=%async_computation.5 | async-start | bytes 1572864 | tf_op jit(solution)/shard_map/slice | solution.py:37
  45.2 5.9 %copy-start.6 = (bf16[8,128,384]{1,2,0:T(8,128)(2,1)}, bf16[8,128,384]{1,2,0:T(8,128)(2,1)S(1)}, u32[]{:S(2)}) copy-start(bf16[8,128,384]{1,2,0:T(8,128)(2,1)S(1)} %copy.114) | copy-start | bytes 2359300
  45.2 5.9 %copy-start.9 = (bf16[128,8,384]{2,1,0:T(8,128)(2,1)S(1)}, bf16[128,8,384]{2,1,0:T(8,128)(2,1)}, u32[]{:S(2)}) copy-start(bf16[128,8,384]{2,1,0:T(8,128)(2,1)} %copy-done.8) | copy-start | bytes 2359300
  118.9 24.7 %all-to-all-start.3 = ((bf16[8,128,384]{2,0,1:T(8,128)(2,1)}), bf16[8,128,384]{2,0,1:T(8,128)(2,1)S(1)}, u32[]{:S(2)}, u32[]{:S(2)}) async-start(bf16[8,128,384]{2,0,1:T(8,128)(2,1)} %copy.88), calls=%async_computation.3 | async-start | bytes 1572864 | tf_op jit(solution)/shard_map/all_to_all | solution.py:61
  130.6 1.7 copy-start.5
  143.5 83.7 %all-to-all-start.1 = ((bf16[8,128,1664]{2,0,1:T(8,128)(2,1)}), bf16[8,128,1664]{2,0,1:T(8,128)(2,1)}, u32[]{:S(2)}, u32[]{:S(2)}) async-start(bf16[8,128,1664]{2,0,1:T(8,128)(2,1)} %copy.79), calls=%async_computation.1 | async-start | bytes 6815744 | tf_op jit(solution)/shard_map/all_to_all | solution.py:61
  149.2 4.3 %copy-start.10 = (bf16[128,8,384]{2,1,0:T(8,128)(2,1)S(1)}, bf16[128,8,384]{2,1,0:T(8,128)(2,1)}, u32[]{:S(2)}) copy-start(bf16[128,8,384]{2,1,0:T(8,128)(2,1)} %copy-done.8) | copy-start | bytes 2359300
  227.3 3.2 %copy-start.3 = (bf16[8,128,2048]{2,1,0:T(8,128)(2,1)S(1)}, bf16[8,128,2048]{2,1,0:T(8,128)(2,1)}, u32[]{:S(2)}) copy-start(bf16[8,128,2048]{2,1,0:T(8,128)(2,1)} %param.4) | copy-start | bytes 12582916
  229.9 1.8 copy-start.2
  230.5 1.7 copy-start.11
  232.2 9.9 %copy-start.7 = (bf16[8,128,384]{1,2,0:T(8,128)(2,1)S(1)}, bf16[8,128,384]{1,2,0:T(8,128)(2,1)}, u32[]{:S(2)}) copy-start(bf16[8,128,384]{1,2,0:T(8,128)(2,1)} %copy-done.6) | copy-start | bytes 2359300
  233.7 25.5 %all-to-all-start.4 = ((f32[2,8,128,128]{3,1,0,2:T(8,128)}), f32[2,8,128,128]{3,1,0,2:T(8,128)S(1)}, u32[]{:S(2)}, u32[]{:S(2)}) async-start(f32[2,8,128,128]{3,1,0,2:T(8,128)} %copy.99), calls=%async_computation.4 | async-start | bytes 2097152 | tf_op jit(solution)/shard_map/all_to_all | solution.py:16
  247.3 12.7 %copy-start.1 = (bf16[8,128,128]{2,1,0:T(8,128)(2,1)S(1)}, bf16[8,128,128]{2,1,0:T(8,128)(2,1)}, u32[]{:S(2)}) copy-start(bf16[8,128,128]{2,1,0:T(8,128)(2,1)} %param.6) | copy-start | bytes 786436
where the time goes:
time: 261 us; the launch traced here: 260 us
  waiting for transfers between devices  157 us (60%)
  local copies, waits for them, and re-layouts  37 us (14%)
  starting transfers between devices  33.5 us (13%)
  matrix products  29.2 us (11%)
    all_to_all x2, waiting for transfers between devices, local(): lax.all_to_all(outgoing, 'block', split_axis=0, concat_axis=1, tiled=True)  78.8 us
    all_to_all x2, waiting for transfers between devices, local(): lax.all_to_all(permuted_grad, 'block', split_axis=1, concat_axis=0, tiled...  74.9 us
    unnamed x27, local copies, waits for them, and re-layouts  15.9 us
    all_to_all x2, starting transfers between devices, local(): lax.all_to_all(outgoing, 'block', split_axis=0, concat_axis=1, tiled=True)  15.4 us
    all_to_all x2, starting transfers between devices, local(): lax.all_to_all(permuted_grad, 'block', split_axis=1, concat_axis=0, tiled...  9.67 us
    dot_general x2, matrix products, local(): jnp.einsum('jit,jik->jkt', forward_received, right_factor, preferred_elem...  8.9 us
    all_to_all x1, starting transfers between devices, dp_reduce_scatter(): lax.all_to_all(terms, 'dp', split_axis=2, concat_axis=0, tiled=True)  8.45 us
    convert_element_type x2, local copies, waits for them, and re-layouts, local(): permuted_grad = jnp.einsum('jkt,jik->jit', mixed_grad, right_factor, pref...  7.3 us
  transfers between devices with their start and end apart: 5, of which 5 were waited for; matrix products, arithmetic and copies ran while one was open for 22% of the time, Pallas kernels for 0%

commit v1 on v0

--- a/solution.py
+++ b/solution.py
@@ -58,7 +58,10 @@
         permuted_grad = jnp.einsum(
             "jkt,jik->jit", mixed_grad, right_factor, preferred_element_type=jnp.float32
         ).astype(jnp.bfloat16)
-        received = lax.all_to_all(permuted_grad, "block", split_axis=1, concat_axis=0, tiled=True)
+        devices = lax.axis_size("block")
+        pieces = jnp.stack(jnp.split(permuted_grad, devices, axis=1), axis=0)
+        pieces = lax.all_to_all(pieces, "block", split_axis=0, concat_axis=0)
+        received = jnp.concatenate(pieces, axis=0)
         branch = jnp.einsum(
             "oit,ico->ict", received, left_factor, preferred_element_type=jnp.float32
         )

time: 261 us -> 265 us (1.015)
  waiting for transfers between devices: 157 us -> 154 us
  starting transfers between devices: 33.5 us -> 36.3 us
  matrix products: 29.2 us -> 31.9 us
    all_to_all x2, waiting for transfers between devices: 78.8 us -> 66.3 us  [local(): lax.all_to_all(outgoing, 'block', split_axis=0, concat_axis=1, tiled=True)]
    all_to_all x2, waiting for transfers between devices: 74.9 us -> 84.5 us  [local(): pieces = lax.all_to_all(pieces, 'block', split_axis=0, concat_axis=0)]
    unnamed x27 -> x45, local copies, waits for them, and re-layouts: 15.9 us -> 25.5 us
    convert_element_type x2 -> x0, local copies, waits for them, and re-layouts: 7.3 us -> none  [local(): permuted_grad = jnp.einsum('jkt,jik->jit', mixed_grad, right_factor, pref...]
    dot_general x2, matrix products: 1.69 us -> 4.76 us  [local(): jnp.einsum('ict,oit->ico', x_group, received, preferred_element_type=jnp....]
    all_to_all x2 -> x0, local copies, waits for them, and re-layouts: 2.76 us -> none  [local(): lax.all_to_all(permuted_grad, 'block', split_axis=1, concat_axis=0, tiled...]
  transfers between devices with their start and end apart: 5 -> 5, of which waited for: 5 -> 4; matrix products, arithmetic and copies ran while one was open for 22% -> 22% of each run, Pallas kernels for 0% -> 0%
where the time goes in v1:
time: 265 us; the launch traced here: 264 us
  waiting for transfers between devices  154 us (58%)
  local copies, waits for them, and re-layouts  37.2 us (14%)
  starting transfers between devices  36.3 us (14%)
  matrix products  31.9 us (12%)
  other arithmetic  3.52 us (1%)
    all_to_all x2, waiting for transfers between devices, local(): pieces = lax.all_to_all(pieces, 'block', split_axis=0, concat_axis=0)  84.5 us
    all_to_all x2, waiting for transfers between devices, local(): lax.all_to_all(outgoing, 'block', split_axis=0, concat_axis=1, tiled=True)  66.3 us
    unnamed x45, local copies, waits for them, and re-layouts  25.5 us
    all_to_all x2, starting transfers between devices, local(): lax.all_to_all(outgoing, 'block', split_axis=0, concat_axis=1, tiled=True)  14.2 us
    all_to_all x2, starting transfers between devices, local(): pieces = lax.all_to_all(pieces, 'block', split_axis=0, concat_axis=0)  11.8 us
    all_to_all x1, starting transfers between devices, dp_reduce_scatter(): lax.all_to_all(terms, 'dp', split_axis=2, concat_axis=0, tiled=True)  10.2 us
    dot_general x2, matrix products, local(): jnp.einsum('jit,jik->jkt', forward_received, right_factor, preferred_elem...  10 us
    dot_general x2, matrix products, local(): jnp.einsum('jit,jkt->jik', forward_received, mixed_grad, preferred_elemen...  5.65 us
  transfers between devices with their start and end apart: 5, of which 4 were waited for; matrix products, arithmetic and copies ran while one was open for 22% of the time, Pallas kernels for 0%

profile of v1, /device:TPU:1, one launch (start us, length us, event | category | flops | bytes accessed | tf_op | source)
XLA Modules:
  0.0 263.9 jit_solution(8018607564177083228)
XLA Ops:
  0.6 3.2 %fusion.12 = bf16[128,8,1664]{2,0,1:T(8,128)(2,1)S(1)} fusion(bf16[8,128,128]{2,1,0:T(8,128)(2,1)} %param.5, bf16[8,128,2048]{2,1,0:T(8,128)(2,1)} %param.4), kind=kOutput, calls=%fused_computation.20 | convolution fusion | flops 437911552 | bytes 7077888 | tf_op jit(solution)/shard_map/ict,ico->oit/dot_general | solution.py:38
  3.8 3.7 %copy.72 = bf16[128,8,1664]{2,1,0:T(8,128)(2,1)} copy(bf16[128,8,1664]{2,0,1:T(8,128)(2,1)S(1)} %fusion.12) | data formatting | bytes 6815744 | tf_op jit(solution)/shard_map/convert_element_type | solution.py:40
  7.5 10.2 %all-to-all-start = ((bf16[128,8,1664]{2,1,0:T(8,128)(2,1)}), bf16[128,8,1664]{2,1,0:T(8,128)(2,1)}, u32[]{:S(2)}, u32[]{:S(2)}) async-start(bf16[128,8,1664]{2,1,0:T(8,128)(2,1)} %copy.72), calls=%async_computation | async-start | bytes 6815744 | tf_op jit(solution)/shard_map/all_to_all | solution.py:41
  17.7 1.5 fusion.30
  19.3 1.4 copy.79
  20.7 4.0 %slice.18 = bf16[8,128,1664]{2,1,0:T(8,128)(2,1)} slice(bf16[8,128,2048]{2,1,0:T(8,128)(2,1)} %param.7), slice={[0:8], [0:128], [0:1664]} | slice | bytes 6815744 | tf_op jit(solution)/shard_map/slice | solution.py:37
  24.6 5.6 %copy.105 = bf16[8,128,1664]{1,2,0:T(8,128)(2,1)} copy(bf16[8,128,1664]{2,1,0:T(8,128)(2,1)} %slice.18) | data formatting | bytes 6815744
  30.2 66.3 %all-to-all-done = bf16[128,8,1664]{2,1,0:T(8,128)(2,1)} async-done(((bf16[128,8,1664]{2,1,0:T(8,128)(2,1)}), bf16[128,8,1664]{2,1,0:T(8,128)(2,1)}, u32[]{:S(2)}, u32[]{:S(2)}) %all-to-all-start) | async-done | bytes 3407904 | tf_op jit(solution)/shard_map/all_to_all | solution.py:41
  96.5 4.0 %all-to-all-start.2 = ((bf16[128,8,384]{2,1,0:T(8,128)(2,1)}), bf16[128,8,384]{2,1,0:T(8,128)(2,1)S(1)}, u32[]{:S(2)}, u32[]{:S(2)}) async-start(bf16[128,8,384]{2,1,0:T(8,128)(2,1)} %copy.79), calls=%async_computation.2 | async-start | bytes 1572864 | tf_op jit(solution)/shard_map/all_to_all | solution.py:41
  100.6 7.6 %fusion = bf16[8,128,1664]{1,2,0:T(8,128)(2,1)S(1)} fusion(bf16[8,128,1664]{1,2,0:T(8,128)(2,1)} %copy.105, bf16[8,128,128]{2,1,0:T(8,128)(2,1)S(1)} %copy-done, bf16[8,16,8,1664]{3,2,0,1:T(8,128)(2,1)} %bitcast.2), kind=kOutput, calls=%fused_computation.4 | convolution fusion | flops 470286336 | bytes 10485760 | tf_op jit(solution)/shard_map/jit,jik->jkt/dot_general | solution.py:44
  108.2 1.1 fusion.13
  109.3 0.7 copy-done.3
  110.0 0.7 fusion.59
  110.7 0.7 fusion.58
  111.4 0.7 fusion.57
  112.1 0.7 fusion.56
  112.8 0.7 fusion.55
  113.5 0.7 fusion.54
  114.2 0.7 fusion.53
  114.9 0.7 fusion.52
  115.6 0.7 fusion.51
  116.3 0.7 fusion.50
  117.0 0.7 fusion.49
  117.7 0.7 fusion.48
  118.4 0.7 fusion.47
  119.1 0.7 fusion.46
  119.8 0.7 fusion.45
  120.5 0.7 fusion.44
  121.2 7.7 %all-to-all-start.1 = ((bf16[16,8,8,1664]{3,2,1,0:T(8,128)(2,1)}), bf16[16,8,8,1664]{3,2,1,0:T(8,128)(2,1)}, u32[]{:S(2)}, u32[]{:S(2)}) async-start(bf16[16,8,8,1664]{3,2,1,0:T(8,128)(2,1)} %fusion.44), calls=%async_computation.1 | async-start | bytes 6815744 | tf_op jit(solution)/shard_map/all_to_all | solution.py:63
  128.9 1.2 copy.106
  130.1 2.5 fusion.21
  132.6 0.5 fusion.31
  133.4 0.9 copy-done.5
  134.3 72.8 %all-to-all-done.1 = bf16[16,8,8,1664]{3,2,1,0:T(8,128)(2,1)} async-done(((bf16[16,8,8,1664]{3,2,1,0:T(8,128)(2,1)}), bf16[16,8,8,1664]{3,2,1,0:T(8,128)(2,1)}, u32[]{:S(2)}, u32[]{:S(2)}) %all-to-all-start.1) | async-done | bytes 3407904 | tf_op jit(solution)/shard_map/all_to_all | solution.py:63
  207.1 4.1 %all-to-all-start.3 = ((bf16[16,8,8,384]{3,2,1,0:T(8,128)(2,1)}), bf16[16,8,8,384]{3,2,1,0:T(8,128)(2,1)S(1)}, u32[]{:S(2)}, u32[]{:S(2)}) async-start(bf16[16,8,8,384]{3,2,1,0:T(8,128)(2,1)} %copy-done.5), calls=%async_computation.3 | async-start | bytes 1572864 | tf_op jit(solution)/shard_map/all_to_all | solution.py:63
  211.2 4.4 %fusion.9 = f32[8,128,128]{1,2,0:T(8,128)S(1)} fusion(bf16[8,128,1664]{1,2,0:T(8,128)(2,1)} %copy-done.3, bf16[8,16,8,1664]{3,2,0,1:T(8,128)(2,1)} %bitcast.2), kind=kOutput, calls=%fused_computation.17 | convolution fusion | flops 436207616 | bytes 7340032 | tf_op jit(solution)/shard_map/jit,jkt->jik/dot_general | solution.py:50
  215.6 1.3 fusion.35
  216.9 3.2 %fusion.15 = f32[8,128,128]{2,1,0:T(8,128)S(1)} fusion(bf16[128,8,1664]{2,1,0:T(8,128)(2,1)} %bitcast.22, bf16[8,128,2048]{2,1,0:T(8,128)(2,1)S(1)} %copy-done.1), kind=kOutput, calls=%fused_computation.23 | convolution fusion | flops 436207616 | bytes 7340032 | tf_op jit(solution)/shard_map/ict,oit->ico/dot_general | solution.py:71
  220.0 11.7 %all-to-all-done.3 = bf16[16,8,8,384]{3,2,1,0:T(8,128)(2,1)S(1)} async-done(((bf16[16,8,8,384]{3,2,1,0:T(8,128)(2,1)}), bf16[16,8,8,384]{3,2,1,0:T(8,128)(2,1)S(1)}, u32[]{:S(2)}, u32[]{:S(2)}) %all-to-all-start.3) | async-done | bytes 786464 | tf_op jit(solution)/shard_map/all_to_all | solution.py:63
  231.7 1.6 fusion.33
  233.3 1.2 pad_maximum_fusion.1
  234.5 1.4 copy.91
  235.9 10.2 %all-to-all-start.4 = ((f32[2,8,128,128]{3,1,0,2:T(8,128)}), f32[2,8,128,128]{3,1,0,2:T(8,128)S(1)}, u32[]{:S(2)}, u32[]{:S(2)}) async-start(f32[2,8,128,128]{3,1,0,2:T(8,128)} %copy.91), calls=%async_computation.4 | async-start | bytes 2097152 | tf_op jit(solution)/shard_map/all_to_all | solution.py:16
  246.5 4.7 %fusion.1 = bf16[8,128,1664]{1,2,0:T(8,128)(2,1)S(1)} fusion(bf16[8,128,1664]{1,2,0:T(8,128)(2,1)} %copy.105, bf16[8,128,128]{2,1,0:T(8,128)(2,1)S(1)} %copy-done.2, bf16[128,8,1664]{2,1,0:T(8,128)(2,1)} %bitcast.22), kind=kOutput, calls=%fused_computation.5 | convolution fusion | flops 441319424 | bytes 10485760 | tf_op jit(solution)/shard_map/oit,ico->ict/dot_general | solution.py:65
  251.2 2.3 pad_maximum_fusion
  253.5 6.4 %copy.93 = bf16[8,128,2048]{2,1,0:T(8,128)(2,1)} copy(bf16[8,128,2048]{1,2,0:T(8,128)(2,1)} %pad_maximum_fusion) | data formatting | bytes 8388608
  259.9 3.2 %all-to-all-done.4 = f32[2,8,128,128]{3,1,0,2:T(8,128)S(1)} async-done(((f32[2,8,128,128]{3,1,0,2:T(8,128)}), f32[2,8,128,128]{3,1,0,2:T(8,128)S(1)}, u32[]{:S(2)}, u32[]{:S(2)}) %all-to-all-start.4) | async-done | bytes 1048608 | tf_op jit(solution)/shard_map/all_to_all | solution.py:16
  263.3 0.6 copy_bitcast_fusion
  (32 shorter events, 0.8 us)
Async XLA Ops:
  0.6 99.9 %copy-start = (bf16[8,128,128]{2,1,0:T(8,128)(2,1)S(1)}, bf16[8,128,128]{2,1,0:T(8,128)(2,1)}, u32[]{:S(2)}) copy-start(bf16[8,128,128]{2,1,0:T(8,128)(2,1)} %param.6) | copy-start | bytes 786436
  7.5 10.2 %copy-start.2 = (bf16[8,128,128]{2,1,0:T(8,128)(2,1)S(1)}, bf16[8,128,128]{2,1,0:T(8,128)(2,1)}, u32[]{:S(2)}) copy-start(bf16[8,128,128]{2,1,0:T(8,128)(2,1)} %param.5) | copy-start | bytes 786436
  7.5 89.0 %all-to-all-start = ((bf16[128,8,1664]{2,1,0:T(8,128)(2,1)}), bf16[128,8,1664]{2,1,0:T(8,128)(2,1)}, u32[]{:S(2)}, u32[]{:S(2)}) async-start(bf16[128,8,1664]{2,1,0:T(8,128)(2,1)} %copy.72), calls=%async_computation | async-start | bytes 6815744 | tf_op jit(solution)/shard_map/all_to_all | solution.py:41
  96.5 24.7 %all-to-all-start.2 = ((bf16[128,8,384]{2,1,0:T(8,128)(2,1)}), bf16[128,8,384]{2,1,0:T(8,128)(2,1)S(1)}, u32[]{:S(2)}, u32[]{:S(2)}) async-start(bf16[128,8,384]{2,1,0:T(8,128)(2,1)} %copy.79), calls=%async_computation.2 | async-start | bytes 1572864 | tf_op jit(solution)/shard_map/all_to_all | solution.py:41
  108.1 1.9 copy-start.3
  121.2 7.8 %slice-start = ((bf16[8,128,2048]{2,1,0:T(8,128)(2,1)}), bf16[8,128,384]{2,1,0:T(8,128)(2,1)S(1)}, s32[]{:S(2)}) async-start(bf16[8,128,2048]{2,1,0:T(8,128)(2,1)} %param.7), calls=%async_computation.5 | async-start | bytes 1572864 | tf_op jit(solution)/shard_map/slice | solution.py:37
  121.2 85.9 %all-to-all-start.1 = ((bf16[16,8,8,1664]{3,2,1,0:T(8,128)(2,1)}), bf16[16,8,8,1664]{3,2,1,0:T(8,128)(2,1)}, u32[]{:S(2)}, u32[]{:S(2)}) async-start(bf16[16,8,8,1664]{3,2,1,0:T(8,128)(2,1)} %fusion.44), calls=%async_computation.1 | async-start | bytes 6815744 | tf_op jit(solution)/shard_map/all_to_all | solution.py:63
  133.4 0.9 copy-start.5
  207.1 24.6 %all-to-all-start.3 = ((bf16[16,8,8,384]{3,2,1,0:T(8,128)(2,1)}), bf16[16,8,8,384]{3,2,1,0:T(8,128)(2,1)S(1)}, u32[]{:S(2)}, u32[]{:S(2)}) async-start(bf16[16,8,8,384]{3,2,1,0:T(8,128)(2,1)} %copy-done.5), calls=%async_computation.3 | async-start | bytes 1572864 | tf_op jit(solution)/shard_map/all_to_all | solution.py:63
  211.2 5.7 %copy-start.1 = (bf16[8,128,2048]{2,1,0:T(8,128)(2,1)S(1)}, bf16[8,128,2048]{2,1,0:T(8,128)(2,1)}, u32[]{:S(2)}) copy-start(bf16[8,128,2048]{2,1,0:T(8,128)(2,1)} %param.4) | copy-start | bytes 12582916
  233.3 12.8 %copy-start.4 = (bf16[8,128,384]{1,2,0:T(8,128)(2,1)S(1)}, bf16[8,128,384]{1,2,0:T(8,128)(2,1)}, u32[]{:S(2)}) copy-start(bf16[8,128,384]{1,2,0:T(8,128)(2,1)} %copy.106) | copy-start | bytes 2359300
  235.9 27.3 %all-to-all-start.4 = ((f32[2,8,128,128]{3,1,0,2:T(8,128)}), f32[2,8,128,128]{3,1,0,2:T(8,128)S(1)}, u32[]{:S(2)}, u32[]{:S(2)}) async-start(f32[2,8,128,128]{3,1,0,2:T(8,128)} %copy.91), calls=%async_computation.4 | async-start | bytes 2097152 | tf_op jit(solution)/shard_map/all_to_all | solution.py:16
